TPU v7x, 128 devices: a whole 4x4x4 slice. The times are simulated.
128 devices in a mesh: lon: 8 (over x, core), lat: 16 (over y, z).
Axes of the slice: x: 4, y: 4, z: 4, core: 2. Of those that a mesh axis runs over, the one named last changes fastest.
Arguments:
- tracers: float32 [2, 20, 1024, 3072], P(None, None, 'lat', 'lon'), may hold values from -6 to 6
- east_velocity: bfloat16 [20, 1024, 3072], P(None, 'lat', 'lon'), may hold values from -3 to 3
- north_velocity: bfloat16 [20, 1024, 3072], P(None, 'lat', 'lon'), may hold values from -3 to 3
- vertical_diffusivity: bfloat16 [20, 1024, 3072], P(None, 'lat', 'lon'), may hold values from 0.049804688 to 5
- depth_levels: int32 [1024, 3072], P('lat', 'lon'), may hold values from 0 to 20
- ocean_blocks: int32 [32, 16], P('lat', 'lon'), may hold values 0 or 1
- forcing: float32 [1024, 3072], P('lat', 'lon'), may hold values from -6 to 6
- surface_coupling: float32 [1024, 3072], P('lat', 'lon'), may hold values from 0.1 to 2
Outputs:
- new_tracers: float32 [2, 20, 1024, 3072], P(None, None, 'lat', 'lon')
- surface_solution: float32 [1024, 3072], P('lat', 'lon')
All inputs are finite; a program needn't handle non-finite values. No bound on the sum of `ocean_blocks` on one device may be relied on, other than what follows from the above.
Results may differ from a plain program's by a relative error of at most 0.0003.
Values sent between devices are 32-bit elements; how exact they have to be, the bound alone decides.
No kernel may reach another device: no remote copies, remote signals or barrier semaphores. Data moves between devices by JAX's collectives and lax.ppermute only.
A program may use at most 192 MiB of HBM per device.

v0:
```python
import jax
import jax.numpy as jnp
from jax import lax
from jax.sharding import PartitionSpec as P

ITERS = 3


advection_rate = 0.25
biharmonic_rate = 0.01
corner_weight = 0.5


def extended_2(block, sides, width, periodic):
    for axis, dim in sides:
        count = lax.axis_size(axis)
        forward = [(i, i + 1) for i in range(count - 1)]
        if periodic:
            forward.append((count - 1, 0))
        backward = [(target, source) for source, target in forward]
        low = lax.ppermute(
            lax.slice_in_dim(block, block.shape[dim] - width, None, axis=dim), axis, forward
        )
        high = lax.ppermute(lax.slice_in_dim(block, 0, width, axis=dim), axis, backward)
        block = jnp.concatenate([low, block, high], axis=dim)
    return block


def from_partner(block, axis, stride):
    count = lax.axis_size(axis)
    route = []
    for low in range(count):
        high = low | 1 << stride
        if high != low and high < count:
            route += [(low, high), (high, low)]
    return lax.ppermute(block, axis, route)


def passed_along(value, axis, steps):
    count = lax.axis_size(axis)
    pairs = [(source, (source + steps) % count) for source in range(count)]
    return lax.ppermute(value, axis, pairs)


def shifted(shard, axis, by):
    count = lax.axis_size(axis)
    pairs = [(i, i + by) for i in range(count) if 0 <= i + by < count]
    return lax.ppermute(shard, axis, pairs)


def window(array, shift_row, shift_col):
    inner_height = array.shape[-2] - 2
    inner_width = array.shape[-1] - 2
    return array[..., shift_row : shift_row + inner_height, shift_col : shift_col + inner_width]


def masked_laplacian(values, wet_mask):
    centre = window(values, 1, 1)
    running = jnp.zeros_like(centre)
    for shift_row, shift_col in ((0, 1), (2, 1), (1, 0), (1, 2)):
        running = running + window(wet_mask, shift_row, shift_col) * (
            window(values, shift_row, shift_col) - centre
        )
    return window(wet_mask, 1, 1) * running


def face_flux(speed_one, speed_two, tracer_one, tracer_two, wet_one, wet_two):
    return 0.5 * (speed_one + speed_two) * 0.5 * (tracer_one + tracer_two) * wet_one * wet_two


def baroclinic(padded):
    tracer = padded[0:2]
    wet_mask = padded[2]
    inner_tracer = tracer[..., 1:-1, 1:-1]
    inner_mask = wet_mask[..., 1:-1, 1:-1]
    east_speed = padded[3][..., 1:-1, 1:-1]
    north_speed = padded[4][..., 1:-1, 1:-1]
    lap_one = masked_laplacian(tracer, wet_mask)
    lap_two = masked_laplacian(lap_one, inner_mask)
    centre = window(inner_tracer, 1, 1)
    wet_centre = window(inner_mask, 1, 1)
    east_flux = face_flux(
        window(east_speed, 1, 1),
        window(east_speed, 1, 2),
        centre,
        window(inner_tracer, 1, 2),
        wet_centre,
        window(inner_mask, 1, 2),
    )
    west_flux = face_flux(
        window(east_speed, 1, 0),
        window(east_speed, 1, 1),
        window(inner_tracer, 1, 0),
        centre,
        window(inner_mask, 1, 0),
        wet_centre,
    )
    north_flux = face_flux(
        window(north_speed, 1, 1),
        window(north_speed, 2, 1),
        centre,
        window(inner_tracer, 2, 1),
        wet_centre,
        window(inner_mask, 2, 1),
    )
    south_flux = face_flux(
        window(north_speed, 0, 1),
        window(north_speed, 1, 1),
        window(inner_tracer, 0, 1),
        centre,
        window(inner_mask, 0, 1),
        wet_centre,
    )
    divergence = east_flux - west_flux + north_flux - south_flux
    return wet_centre * (centre - advection_rate * divergence - biharmonic_rate * lap_two)


def vertical_mix(values, wet_mask, diffusivity):
    level_count = wet_mask.shape[0]
    zeros_plane = jnp.zeros_like(wet_mask[0])
    coupling = (
        [zeros_plane]
        + [diffusivity[k] * wet_mask[k] * wet_mask[k - 1] for k in range(1, level_count)]
        + [zeros_plane]
    )
    upper_ratio = []
    reduced = []
    for k in range(level_count):
        diagonal = 1.0 + coupling[k] + coupling[k + 1]
        if k == 0:
            divisor = diagonal
            source = values[:, 0]
        else:
            divisor = diagonal + coupling[k] * upper_ratio[k - 1]
            source = values[:, k] + coupling[k] * reduced[k - 1]
        upper_ratio.append(-coupling[k + 1] / divisor)
        reduced.append(source / divisor)
    result = [reduced[-1]]
    for k in range(level_count - 2, -1, -1):
        result.insert(0, reduced[k] - upper_ratio[k] * result[0])
    return jnp.stack(result, axis=1)


def nine_point(padded, wet_surface, centre_weight):
    centre = window(padded, 1, 1)
    edges = (
        window(padded, 0, 1) + window(padded, 2, 1) + window(padded, 1, 0) + window(padded, 1, 2)
    )
    corners = (
        window(padded, 0, 0) + window(padded, 0, 2) + window(padded, 2, 0) + window(padded, 2, 2)
    )
    return wet_surface * (centre_weight * centre - edges - corner_weight * corners)


def clinic_extend(stacked, fold_signs):
    row_count = stacked.shape[2]
    widened = extended_2(stacked, (("lon", 3),), 2, True)
    extended = extended_2(widened, (("lat", 2),), 2, False)
    top_rows = widened[:, :, row_count - 2 :, :]
    for bit in range(lax.axis_size("lon").bit_length() - 1):
        top_rows = from_partner(top_rows, "lon", bit)
    northern = jnp.flip(top_rows, axis=(2, 3)) * fold_signs
    at_top = lax.axis_index("lat") == lax.axis_size("lat") - 1
    ghost_rows = jnp.where(at_top, northern, extended[:, :, row_count + 2 :, :])
    return jnp.concatenate([extended[:, :, : row_count + 2, :], ghost_rows], axis=2)


def strip_pad(surface_field):
    lon_index = lax.axis_index("lon")
    lon_count = lax.axis_size("lon")
    first_row = surface_field[0:1, :]
    last_row = surface_field[-1:, :]
    following = passed_along(first_row, "lon", -1)
    following_far = shifted(following, "lat", -1)
    preceding = passed_along(last_row, "lon", 1)
    preceding_far = shifted(preceding, "lat", 1)
    above_row = jnp.where(lon_index == lon_count - 1, following_far, following)
    below_row = jnp.where(lon_index == 0, preceding_far, preceding)
    top_strip = jnp.logical_and(
        lon_index == lon_count - 1, lax.axis_index("lat") == lax.axis_size("lat") - 1
    )
    above_row = jnp.where(top_strip, jnp.flip(last_row, axis=1), above_row)
    extended = jnp.concatenate([below_row, surface_field, above_row], axis=0)
    return jnp.concatenate([extended[:, -1:], extended, extended[:, :1]], axis=1)


def residual_total(residual, precond):
    return lax.psum(jnp.sum(residual * precond), ("lon", "lat"))


def solve(surface_source, wet_surface, centre_weight, padder):

    def precondition(residual):
        return wet_surface * residual / centre_weight

    solution = jnp.zeros_like(surface_source)
    residual = surface_source
    precond = precondition(residual)
    direction = precond
    resid_dot = residual_total(residual, precond)
    for iteration in range(ITERS):
        operator_image = nine_point(padder(direction), wet_surface, centre_weight)
        step_size = resid_dot / lax.psum(jnp.sum(direction * operator_image), ("lon", "lat"))
        solution = solution + step_size * direction
        if iteration + 1 < ITERS:
            residual = residual - step_size * operator_image
            precond = precondition(residual)
            dot_next = residual_total(residual, precond)
            direction = precond + dot_next / resid_dot * direction
            resid_dot = dot_next
    return solution


def shards(
    tracers,
    east_velocity,
    north_velocity,
    vertical_diffusivity,
    depth_levels,
    ocean_blocks,
    forcing,
    surface_coupling,
):
    level_count = tracers.shape[1]
    row_count = tracers.shape[2]
    col_count = tracers.shape[3]
    ocean_cells = jnp.repeat(
        jnp.repeat(ocean_blocks, row_count // ocean_blocks.shape[0], axis=0),
        col_count // ocean_blocks.shape[1],
        axis=1,
    ).astype(jnp.float32)
    level_index = lax.broadcasted_iota(jnp.int32, (level_count, row_count, col_count), 0)
    wet_mask = jnp.where(
        level_index < depth_levels[None], ocean_cells[None], jnp.zeros_like(ocean_cells)[None]
    )
    east_float = east_velocity.astype(jnp.float32)
    north_float = north_velocity.astype(jnp.float32)
    stacked = jnp.concatenate(
        [tracers, wet_mask[None], east_float[None], north_float[None]], axis=0
    )
    fold_signs = jnp.array([1.0, 1.0, 1.0, -1.0, -1.0], jnp.float32).reshape(5, 1, 1, 1)
    padded = clinic_extend(stacked, fold_signs)
    provisional = baroclinic(padded)
    new_tracers = vertical_mix(provisional, wet_mask, vertical_diffusivity.astype(jnp.float32))
    wet_surface = wet_mask[0]
    surface_source = wet_surface * (forcing + jnp.mean(new_tracers[0] - new_tracers[1], axis=0))
    centre_weight = 6.0 + surface_coupling
    relaid = lax.all_to_all(
        jnp.stack([surface_source, wet_surface, centre_weight]),
        "lon",
        split_axis=1,
        concat_axis=2,
        tiled=True,
    )
    strip_solution = solve(relaid[0], relaid[1], relaid[2], strip_pad)
    solution = lax.all_to_all(strip_solution, "lon", split_axis=1, concat_axis=0, tiled=True)
    return (new_tracers, solution)


def solution(mesh):
    placed = (
        P(None, None, "lat", "lon"),
        P(None, "lat", "lon"),
        P(None, "lat", "lon"),
        P(None, "lat", "lon"),
        P("lat", "lon"),
        P("lat", "lon"),
        P("lat", "lon"),
        P("lat", "lon"),
    )
    return jax.shard_map(
        shards,
        mesh=mesh,
        in_specs=placed,
        out_specs=(P(None, None, "lat", "lon"), P("lat", "lon")),
        check_vma=False,
    )
```

profile of v0, /device:TPU:1, one launch (start us, length us, event | category | flops | bytes accessed | tf_op | source)
XLA Modules:
  0.0 688.3 jit_solution(2396863528342615531)
XLA Ops:
  1.8 2.1 bitcast_convert_fusion
  4.5 3.4 pad_maximum_fusion.24
  7.9 3.7 copy.355
  13.0 2.6 copy.354
  17.8 2.4 fusion.40
  34.2 2.6 copy.278
  36.8 3.4 copy.277
  40.2 3.1 pad_maximum_fusion.31
  45.5 2.1 add_bitcast_fusion.1
  50.6 4.3 collective-permute-start.2
  57.1 4.5 collective-permute-done.4
  61.6 2.5 collective-permute-start.5
  71.6 1.7 copy.303
  74.9 1.7 copy.299
  98.5 1.7 copy.327
  103.5 1.7 copy.322
  132.9 1.7 copy.337
  161.6 1.7 copy.349
  164.0 2.1 copy.284
  166.1 2.1 copy.281
  168.2 3.8 reverse
  173.8 13.5 %pad_maximum_fusion = f32[5,20,68,388]{3,2,1,0:T(8,128)S(1)} fusion(f32[5,20,2,388]{3,2,1,0:T(2,128)S(1)} %copy_select_fusion, f32[5,20,64,2]{3,2,1,0:T(8,128)S(1)} %copy.278, f32[1,20,64,384]{3,2,1,0:T(8,128)} %copy-done.6, f32[1,20,64,384]{3,2,1,0:T(8,128)} %copy-done.8, f32[1,20,64,384]{3,2,1,0:T(8,128)} %copy-done.10, f32[2,20,64,384]{3,2,1,0:T(8,128)} %param.9, ...), kind=kLoop, calls=%fused_computation | loop fusion | flops 18468800 | bytes 21107200 | tf_op jit(solution)/shard_map/concatenate | solution.py:165
  187.3 4.1 slice_bitcast_fusion.1
  191.3 2.9 copy-done
  194.2 8.3 %fusion.168 = (f32[20,66,386]{2,1,0:T(8,128)}, f32[20,66,386]{2,1,0:T(8,128)}, f32[20,66,386]{2,1,0:T(8,128)}, f32[20,66,386]{2,1,0:T(8,128)}, f32[20,66,386]{2,1,0:T(8,128)}) fusion(f32[20,68,388]{2,1,0:T(8,128)S(1)} %get-tuple-element.77), kind=kLoop, calls=%fused_computation.368 | loop fusion | bytes 20380800 | tf_op jit(solution)/shard_map/slice | solution.py:75
  202.5 6.3 fusion.167
  208.9 7.8 %fusion.43 = (f32[20,64,384]{2,1,0:T(8,128)}, f32[20,64,384]{2,1,0:T(8,128)}) fusion(f32[20,68,388]{2,1,0:T(8,128)} %get-tuple-element.76), kind=kLoop, calls=%fused_computation.83 | loop fusion | flops 1966080 | bytes 9830400 | tf_op jit(solution)/shard_map/mul | solution.py:68
  216.6 3.6 fusion.45
  221.7 19.7 %fusion.2 = f32[2,20,66,386]{3,2,1,0:T(8,128)} fusion(f32[5,20,68,388]{3,2,1,0:T(8,128)} %copy-done, f32[5,20,2,388]{3,2,1,0:T(2,128)S(1)} %copy-done.16, f32[5,20,64,2]{3,2,1,0:T(8,128)S(1)} %copy-done.4, f32[5,20,64,2]{3,2,1,0:T(8,128)S(1)} %copy-done.5, f32[1,20,64,384]{3,2,1,0:T(8,128)S(1)} %copy-done.7, f32[1,20,64,384]{3,2,1,0:T(8,128)S(1)} %copy-done.9, ...), kind=kLoop, calls=%fused_computation.4 | loop fusion | flops 24456960 | bytes 37048640 | tf_op jit(solution)/shard_map/mul | solution.py:64
  241.4 33.2 %fusion.15 = f32[2,20,64,384]{3,2,1,0:T(8,128)} fusion(f32[2,20,66,386]{3,2,1,0:T(8,128)} %fusion.2, f32[2,20,64,384]{3,2,1,0:T(8,128)} %param.9, f32[5,20,2,388]{3,2,1,0:T(2,128)} %copy.284, f32[5,20,64,2]{3,2,1,0:T(8,128)S(1)} %copy-done.4, f32[5,20,64,2]{3,2,1,0:T(8,128)} %copy.277, f32[1,20,64,384]{3,2,1,0:T(8,128)} %copy-done.6, ...), kind=kLoop, calls=%fused_computation.31 | loop fusion | flops 55050240 | bytes 51841280 | tf_op jit(solution)/shard_map/mul | solution.py:115
  274.7 4.8 subtract_dynamic-update-slice_fusion
  282.8 1.9 copy-done.17
  286.4 11.8 %all_to_all.34 = f32[3,64,384]{2,0,1:T(4,128)S(1)} all-to-all(f32[3,64,384]{2,0,1:T(4,128)S(1)} %copy.351), channel_id=1, replica_groups=mesh['lon'=8,'lat'=16] {'lon'}, dimensions={1} | all-to-all | bytes 589824 | tf_op jit(solution)/shard_map/all_to_all | solution.py:248
  301.0 3.5 collective-permute-start.8
  304.5 2.1 rev.15
  308.0 3.3 collective-permute-done.10
  312.3 69.1 %all-reduce = (f32[]{:T(128)}, f32[]{:T(128)}) all-reduce(f32[]{:T(128)} %get-tuple-element.113, f32[]{:T(128)} %get-tuple-element.14), channel_id=1, replica_groups=mesh['lon'=8,'lat'=16] {'lon','lat'}, use_global_device_ids=true, to_apply=%region_2.3 | all-reduce | flops 2 | bytes 16 | tf_op jit(solution)/shard_map/psum | solution.py:188
  383.4 63.8 %psum.44 = f32[]{:T(128)} all-reduce(f32[]{:T(128)} %get-tuple-element.12), channel_id=1, replica_groups=mesh['lon'=8,'lat'=16] {'lon','lat'}, use_global_device_ids=true, to_apply=%region_6.7 | all-reduce | flops 1 | bytes 8 | tf_op jit(solution)/shard_map/psum | solution.py:188
  450.2 1.9 collective-permute-start.12
  452.1 2.1 rev.16
  455.5 3.1 collective-permute-done.14
  459.6 70.1 %psum.45 = f32[]{:T(128)} all-reduce(f32[]{:T(128)} %get-tuple-element.10), channel_id=1, replica_groups=mesh['lon'=8,'lat'=16] {'lon','lat'}, use_global_device_ids=true, to_apply=%region_8.9 | all-reduce | flops 1 | bytes 8 | tf_op jit(solution)/shard_map/psum | solution.py:203
  531.7 63.0 %psum.46 = f32[]{:T(128)} all-reduce(f32[]{:T(128)} %get-tuple-element.8), channel_id=1, replica_groups=mesh['lon'=8,'lat'=16] {'lon','lat'}, use_global_device_ids=true, to_apply=%region_10.11 | all-reduce | flops 1 | bytes 8 | tf_op jit(solution)/shard_map/psum | solution.py:188
  598.2 1.8 collective-permute-start.16
  600.0 2.1 rev.17
  603.4 3.1 collective-permute-done.18
  607.6 68.8 %psum.47 = f32[]{:T(128)} all-reduce(f32[]{:T(128)} %fusion.97), channel_id=1, replica_groups=mesh['lon'=8,'lat'=16] {'lon','lat'}, use_global_device_ids=true, to_apply=%region_12.13 | all-reduce | flops 1 | bytes 8 | tf_op jit(solution)/shard_map/psum | solution.py:203
  677.7 9.5 %all_to_all.35 = f32[8,8,384]{2,0,1:T(8,128)S(1)} all-to-all(f32[8,8,384]{2,0,1:T(8,128)S(1)} %bitcast.182), channel_id=1, replica_groups=mesh['lon'=8,'lat'=16] {'lon'}, dimensions={1} | all-to-all | bytes 196608 | tf_op jit(solution)/shard_map/all_to_all | solution.py:256
  (303 shorter events, 139.3 us)
Async XLA Ops:
  11.6 22.6 %collective-permute-start.1 = (f32[5,20,64,2]{2,1,3,0:T(8,128)}, f32[5,20,64,2]{2,1,3,0:T(8,128)}, u32[]{:S(2)}, u32[]{:S(2)}) collective-permute-start(f32[5,20,64,2]{2,1,3,0:T(8,128)} %copy.355), channel_id=1, source_target_pairs={{16,0},{32,16},{48,32},{64,48},{80,64},{96,80},{112,96},{0,112},{1... | collective-permute-start | bytes 153608 | tf_op jit(solution)/shard_map/ppermute | solution.py:24
  15.5 21.3 %collective-permute-start = (f32[5,20,64,2]{2,1,3,0:T(8,128)}, f32[5,20,64,2]{2,1,3,0:T(8,128)}, u32[]{:S(2)}, u32[]{:S(2)}) collective-permute-start(f32[5,20,64,2]{2,1,3,0:T(8,128)} %copy.354), channel_id=1, source_target_pairs={{0,16},{16,32},{32,48},{48,64},{64,80},{80,96},{96,112},{112,0},{1... | collective-permute-start | bytes 153608 | tf_op jit(solution)/shard_map/ppermute | solution.py:21
  23.3 9.9 %copy-start.13 = (f32[20,64,384]{1,2,0:T(8,128)}, f32[20,64,384]{1,2,0:T(8,128)S(1)}, u32[]{:S(2)}) copy-start(f32[20,64,384]{1,2,0:T(8,128)S(1)} %convert_element_type.23) | copy-start | bytes 5898244
  36.8 136.9 %copy-start.3 = (f32[5,20,64,2]{3,2,1,0:T(8,128)}, f32[5,20,64,2]{3,2,1,0:T(8,128)S(1)}, u32[]{:S(2)}) copy-start(f32[5,20,64,2]{3,2,1,0:T(8,128)S(1)} %copy.278) | copy-start | bytes 153604
  40.2 7.4 %copy-start.22 = (f32[1,64,384]{1,2,0:T(8,128)S(1)}, f32[1,64,384]{1,2,0:T(8,128)}, u32[]{:S(2)}) copy-start(f32[1,64,384]{1,2,0:T(8,128)} %copy-done.21) | copy-start | bytes 294916
  40.2 7.4 %copy-start.24 = (f32[1,64,384]{1,2,0:T(8,128)S(1)}, f32[1,64,384]{1,2,0:T(8,128)}, u32[]{:S(2)}) copy-start(f32[1,64,384]{1,2,0:T(8,128)} %copy-done.23) | copy-start | bytes 294916
  40.2 7.5 %copy-start.34 = (f32[1,64,384]{1,2,0:T(8,128)S(1)}, f32[1,64,384]{1,2,0:T(8,128)}, u32[]{:S(2)}) copy-start(f32[1,64,384]{1,2,0:T(8,128)} %copy-done.33) | copy-start | bytes 294916
  40.2 7.5 %copy-start.36 = (f32[1,64,384]{1,2,0:T(8,128)S(1)}, f32[1,64,384]{1,2,0:T(8,128)}, u32[]{:S(2)}) copy-start(f32[1,64,384]{1,2,0:T(8,128)} %copy-done.35) | copy-start | bytes 294916
  40.2 7.5 %copy-start.49 = (f32[1,64,384]{1,2,0:T(8,128)S(1)}, f32[1,64,384]{1,2,0:T(8,128)}, u32[]{:S(2)}) copy-start(f32[1,64,384]{1,2,0:T(8,128)} %get-tuple-element.56) | copy-start | bytes 294916
  40.2 7.5 %copy-start.50 = (f32[1,64,384]{1,2,0:T(8,128)S(1)}, f32[1,64,384]{1,2,0:T(8,128)}, u32[]{:S(2)}) copy-start(f32[1,64,384]{1,2,0:T(8,128)} %get-tuple-element.60) | copy-start | bytes 294916
  43.4 6.2 copy-start.26
  43.4 6.2 copy-start.28
  43.4 6.2 copy-start.30
  43.4 6.2 copy-start.32
  43.4 6.2 copy-start.51
  43.4 6.2 copy-start.52
  44.3 4.4 collective-permute-start.3
  47.6 16.5 %copy-start.43 = (f32[1,64,384]{1,2,0:T(8,128)}, f32[1,64,384]{1,2,0:T(8,128)S(1)}, u32[]{:S(2)}) copy-start(f32[1,64,384]{1,2,0:T(8,128)S(1)} %get-tuple-element.70) | copy-start | bytes 294916
  47.6 17.2 %copy-start.44 = (f32[1,64,384]{1,2,0:T(8,128)}, f32[1,64,384]{1,2,0:T(8,128)S(1)}, u32[]{:S(2)}) copy-start(f32[1,64,384]{1,2,0:T(8,128)S(1)} %get-tuple-element.71) | copy-start | bytes 294916
  47.6 17.2 %copy-start.45 = (f32[1,64,384]{1,2,0:T(8,128)}, f32[1,64,384]{1,2,0:T(8,128)S(1)}, u32[]{:S(2)}) copy-start(f32[1,64,384]{1,2,0:T(8,128)S(1)} %get-tuple-element.72) | copy-start | bytes 294916
  48.8 12.9 %collective-permute-start.4 = (f32[5,20,2,388]{3,1,2,0:T(8,128)S(1)}, f32[5,20,2,388]{3,1,2,0:T(8,128)}, u32[]{:S(2)}, u32[]{:S(2)}) collective-permute-start(f32[5,20,2,388]{3,1,2,0:T(8,128)S(1)} %collective-permute-done.3), channel_id=1, source_target_pairs={{0,32},{32,0},{16,48},{48,16},{64,96},{96,64},{80,112},{112,80},{1... | collective-permute-start | bytes 931208 | tf_op jit(solution)/shard_map/ppermute | solution.py:36
  50.6 113.4 %collective-permute-start.2 = (f32[5,20,2,388]{3,1,2,0:T(8,128)}, f32[5,20,2,388]{3,1,2,0:T(8,128)}, u32[]{:S(2)}, u32[]{:S(2)}) collective-permute-start(f32[5,20,2,388]{3,1,2,0:T(8,128)} %copy.279), channel_id=1, source_target_pairs={{0,1},{1,2},{2,3},{3,4},{4,5},{5,6},{6,7},{7,8},{8,9},{9,10},{10,1... | collective-permute-start | bytes 931208 | tf_op jit(solution)/shard_map/ppermute | solution.py:21
  55.8 116.2 %collective-permute-start.6 = (f32[5,20,2,388]{3,1,2,0:T(8,128)}, f32[5,20,2,388]{3,1,2,0:T(8,128)}, u32[]{:S(2)}, u32[]{:S(2)}) collective-permute-start(f32[5,20,2,388]{3,1,2,0:T(8,128)} %copy.282), channel_id=1, source_target_pairs={{1,0},{2,1},{3,2},{4,3},{5,4},{6,5},{7,6},{8,7},{9,8},{10,9},{11,1... | collective-permute-start | bytes 931208 | tf_op jit(solution)/shard_map/ppermute | solution.py:24
  61.6 104.5 %collective-permute-start.5 = (f32[5,20,2,388]{3,1,2,0:T(8,128)}, f32[5,20,2,388]{3,1,2,0:T(8,128)}, u32[]{:S(2)}, u32[]{:S(2)}) collective-permute-start(f32[5,20,2,388]{3,1,2,0:T(8,128)} %collective-permute-done.4), channel_id=1, source_target_pairs={{0,64},{64,0},{16,80},{80,16},{32,96},{96,32},{48,112},{112,48},{1... | collective-permute-start | bytes 931208 | tf_op jit(solution)/shard_map/ppermute | solution.py:36
  132.9 21.9 %copy-start.40 = (f32[1,64,384]{1,2,0:T(8,128)S(1)}, f32[1,64,384]{1,2,0:T(8,128)}, u32[]{:S(2)}) copy-start(f32[1,64,384]{1,2,0:T(8,128)} %copy-done.39) | copy-start | bytes 294916
  138.0 34.1 %copy-start.70 = (f32[5]{0:T(128)S(1)}, f32[5]{0:T(128)}, u32[]{:S(2)}) copy-start(f32[5]{0:T(128)} %constant.38.clone) | copy-start | bytes 64
  173.8 13.5 %copy-start.15 = (f32[5,20,2,388]{3,2,1,0:T(2,128)}, f32[5,20,2,388]{3,2,1,0:T(2,128)S(1)}, u32[]{:S(2)}) copy-start(f32[5,20,2,388]{3,2,1,0:T(2,128)S(1)} %copy_select_fusion) | copy-start | bytes 931204
  187.2 6.9 %copy-start = (f32[5,20,68,388]{3,2,1,0:T(8,128)}, f32[5,20,68,388]{3,2,1,0:T(8,128)S(1)}, u32[]{:S(2)}) copy-start(f32[5,20,68,388]{3,2,1,0:T(8,128)S(1)} %pad_maximum_fusion) | copy-start | bytes 31660804
  208.8 7.8 %copy-start.11 = (f32[20,68,388]{2,1,0:T(8,128)S(1)}, f32[20,68,388]{2,1,0:T(8,128)}, u32[]{:S(2)}) copy-start(f32[20,68,388]{2,1,0:T(8,128)} %get-tuple-element.75) | copy-start | bytes 6332164
  208.8 11.4 %copy-start.5 = (f32[5,20,64,2]{3,2,1,0:T(8,128)S(1)}, f32[5,20,64,2]{3,2,1,0:T(8,128)}, u32[]{:S(2)}) copy-start(f32[5,20,64,2]{3,2,1,0:T(8,128)} %copy.277) | copy-start | bytes 153604
  208.8 11.4 %copy-start.9 = (f32[1,20,64,384]{3,2,1,0:T(8,128)S(1)}, f32[1,20,64,384]{3,2,1,0:T(8,128)}, u32[]{:S(2)}) copy-start(f32[1,20,64,384]{3,2,1,0:T(8,128)} %copy-done.8) | copy-start | bytes 5898244
  208.8 11.4 %copy-start.16 = (f32[5,20,2,388]{3,2,1,0:T(2,128)S(1)}, f32[5,20,2,388]{3,2,1,0:T(2,128)}, u32[]{:S(2)}) copy-start(f32[5,20,2,388]{3,2,1,0:T(2,128)} %copy-done.15) | copy-start | bytes 931204
  241.4 33.2 %copy-start.54 = (f32[64,384]{1,0:T(8,128)S(1)}, f32[64,384]{1,0:T(8,128)}, u32[]{:S(2)}) copy-start(f32[64,384]{1,0:T(8,128)} %copy.347) | copy-start | bytes 294916
  241.4 33.3 %copy-start.55 = (f32[64,384]{1,0:T(8,128)S(1)}, f32[64,384]{1,0:T(8,128)}, u32[]{:S(2)}) copy-start(f32[64,384]{1,0:T(8,128)} %copy.346) | copy-start | bytes 294916
  280.6 5.4 copy-start.66
  280.6 5.4 copy-start.67
  299.1 1.9 collective-permute-start.7
  300.2 6.5 collective-permute-start.9
  301.0 7.0 %collective-permute-start.8 = (f32[1,3072]{1,0:T(1,128)S(1)}, f32[1,3072]{1,0:T(1,128)S(1)}, u32[]{:S(2)}, u32[]{:S(2)}) collective-permute-start(f32[1,3072]{1,0:T(1,128)S(1)} %collective-permute-done.7), channel_id=1, source_target_pairs={{0,1},{1,2},{2,3},{3,4},{4,5},{5,6},{6,7},{7,8},{8,9},{9,10},{10,1... | collective-permute-start | bytes 36872 | tf_op jit(solution)/shard_map/ppermute | solution.py:48
  306.6 4.6 collective-permute-start.10
  448.6 1.6 collective-permute-start.11
  448.8 5.4 collective-permute-start.13
  450.2 5.3 collective-permute-start.12
  454.2 4.4 collective-permute-start.14
  596.0 2.2 collective-permute-start.15
  597.3 4.8 collective-permute-start.17
  598.2 5.3 collective-permute-start.16
  602.1 4.4 collective-permute-start.18
  (42 other events, 129.3 us)
where the time goes:
time: 698 us; the launch traced here: 688 us
  blocking collectives  356 us (51%)
  local copies, waits for them, and re-layouts  159 us (23%)
  other arithmetic  122 us (17%)
  starting transfers between devices  26.4 us (4%)
  waiting for transfers between devices  16.4 us (2%)
  between operations  8.75 us (1%)
    psum x3, blocking collectives, residual_total(): return lax.psum(jnp.sum(residual * precond), ('lon', 'lat'))  196 us
    psum x2, blocking collectives, solve(): lax.psum(jnp.sum(direction * operator_image), ('lon', 'lat'))  139 us
    mul x1, other arithmetic, baroclinic(): wet_centre * (centre - advection_rate * divergence - biharmonic_rate * la...  33.2 us
    mul x19, local copies, waits for them, and re-layouts, vertical_mix(): source = values[:, k] + coupling[k] * reduced[k - 1]  32 us
    mul x19, local copies, waits for them, and re-layouts, vertical_mix(): result.insert(0, reduced[k] - upper_ratio[k] * result[0])  31.9 us
    div x20, local copies, waits for them, and re-layouts, vertical_mix(): reduced.append(source / divisor)  31.8 us
    unnamed x163, local copies, waits for them, and re-layouts  24.9 us
    mul x1, other arithmetic, masked_laplacian(): return window(wet_mask, 1, 1) * running  19.7 us
  transfers between devices with their start and end apart: 19, of which 7 were waited for; matrix products, arithmetic and copies ran while one was open for 20% of the time, Pallas kernels for 0%

commit v1 on v0

--- a/solution.py
+++ b/solution.py
@@ -184,8 +184,18 @@
     return jnp.concatenate([extended[:, -1:], extended, extended[:, :1]], axis=1)
 
 
+def butterfly_sum(value):
+    for axis in ("lon", "lat"):
+        count = lax.axis_size(axis)
+        bit = 1
+        while bit < count:
+            value = value + lax.ppermute(value, axis, [(i, i ^ bit) for i in range(count)])
+            bit <<= 1
+    return value
+
+
 def residual_total(residual, precond):
-    return lax.psum(jnp.sum(residual * precond), ("lon", "lat"))
+    return butterfly_sum(jnp.sum(residual * precond))
 
 
 def solve(surface_source, wet_surface, centre_weight, padder):
@@ -197,10 +207,16 @@
     residual = surface_source
     precond = precondition(residual)
     direction = precond
-    resid_dot = residual_total(residual, precond)
+    resid_dot = None
     for iteration in range(ITERS):
         operator_image = nine_point(padder(direction), wet_surface, centre_weight)
-        step_size = resid_dot / lax.psum(jnp.sum(direction * operator_image), ("lon", "lat"))
+        curvature = jnp.sum(direction * operator_image)
+        if resid_dot is None:
+            both = butterfly_sum(jnp.stack([jnp.sum(residual * precond), curvature]))
+            resid_dot, curvature = both[0], both[1]
+        else:
+            curvature = butterfly_sum(curvature)
+        step_size = resid_dot / curvature
         solution = solution + step_size * direction
         if iteration + 1 < ITERS:
             residual = residual - step_size * operator_image

time: 698 us -> 538 us (0.77)
  blocking collectives: 356 us -> 26.8 us
  starting transfers between devices: 26.4 us -> 135 us
  waiting for transfers between devices: 16.4 us -> 57.6 us
  between operations: 8.75 us -> 22.9 us
    psum x5 -> x0, blocking collectives: 335 us -> none  [the longest x3 196 us: residual_total(): return lax.psum(jnp.sum(residual * precond), ('lon', 'lat'))]
    ppermute x0 -> x35, starting transfers between devices: none -> 93.4 us  [butterfly_sum(): lax.ppermute(value, axis, [(i, i ^ bit) for i in range(count)])]
    ppermute x0 -> x35, waiting for transfers between devices: none -> 41 us  [butterfly_sum(): lax.ppermute(value, axis, [(i, i ^ bit) for i in range(count)])]
    ppermute x6, starting transfers between devices: 3.36 us -> 16.3 us  [passed_along(): return lax.ppermute(value, axis, pairs)]
  transfers between devices with their start and end apart: 19 -> 54, of which waited for: 7 -> 42; matrix products, arithmetic and copies ran while one was open for 20% -> 27% of each run, Pallas kernels for 0% -> 0%
where the time goes in v1:
time: 538 us; the launch traced here: 529 us
  local copies, waits for them, and re-layouts  159 us (30%)
  starting transfers between devices  135 us (25%)
  other arithmetic  127 us (24%)
  waiting for transfers between devices  57.6 us (11%)
  blocking collectives  26.8 us (5%)
  between operations  22.9 us (4%)
    ppermute x35, starting transfers between devices, butterfly_sum(): lax.ppermute(value, axis, [(i, i ^ bit) for i in range(count)])  93.4 us
    ppermute x35, waiting for transfers between devices, butterfly_sum(): lax.ppermute(value, axis, [(i, i ^ bit) for i in range(count)])  41 us
    mul x1, other arithmetic, baroclinic(): wet_centre * (centre - advection_rate * divergence - biharmonic_rate * la...  33.9 us
    mul x19, local copies, waits for them, and re-layouts, vertical_mix(): source = values[:, k] + coupling[k] * reduced[k - 1]  32 us
    mul x19, local copies, waits for them, and re-layouts, vertical_mix(): result.insert(0, reduced[k] - upper_ratio[k] * result[0])  32 us
    div x20, local copies, waits for them, and re-layouts, vertical_mix(): reduced.append(source / divisor)  31.9 us
    unnamed x163, local copies, waits for them, and re-layouts  24.9 us
    mul x1, other arithmetic, masked_laplacian(): return window(wet_mask, 1, 1) * running  19.5 us
  transfers between devices with their start and end apart: 54, of which 42 were waited for; matrix products, arithmetic and copies ran while one was open for 27% of the time, Pallas kernels for 0%

profile of v1, /device:TPU:1, one launch (start us, length us, event | category | flops | bytes accessed | tf_op | source)
XLA Modules:
  0.0 528.5 jit_solution(9503101285327587870)
XLA Ops:
  4.5 3.4 pad_maximum_fusion.24
  7.9 3.7 copy.355
  34.2 2.6 copy.278
  36.8 3.4 copy.277
  40.3 3.1 pad_maximum_fusion.31
  50.7 4.4 collective-permute-start.2
  57.3 4.4 collective-permute-done.4
  168.4 3.9 reverse
  173.9 13.5 %pad_maximum_fusion = f32[5,20,68,388]{3,2,1,0:T(8,128)S(1)} fusion(f32[5,20,2,388]{3,2,1,0:T(2,128)S(1)} %copy_select_fusion, f32[5,20,64,2]{3,2,1,0:T(8,128)S(1)} %copy.278, f32[1,20,64,384]{3,2,1,0:T(8,128)} %copy-done.6, f32[1,20,64,384]{3,2,1,0:T(8,128)} %copy-done.8, f32[1,20,64,384]{3,2,1,0:T(8,128)} %copy-done.10, f32[2,20,64,384]{3,2,1,0:T(8,128)} %param.9, ...), kind=kLoop, calls=%fused_computation | loop fusion | flops 18468800 | bytes 21107200 | tf_op jit(solution)/shard_map/concatenate | solution.py:165
  187.4 4.1 slice_bitcast_fusion.1
  191.5 2.8 copy-done
  194.3 8.4 %fusion.168 = (f32[20,66,386]{2,1,0:T(8,128)}, f32[20,66,386]{2,1,0:T(8,128)}, f32[20,66,386]{2,1,0:T(8,128)}, f32[20,66,386]{2,1,0:T(8,128)}, f32[20,66,386]{2,1,0:T(8,128)}) fusion(f32[20,68,388]{2,1,0:T(8,128)S(1)} %get-tuple-element.75), kind=kLoop, calls=%fused_computation.369 | loop fusion | bytes 20380800 | tf_op jit(solution)/shard_map/slice | solution.py:75
  202.8 6.4 %fusion.167 = (f32[20,64,384]{2,1,0:T(8,128)}, f32[20,64,384]{2,1,0:T(8,128)}, f32[20,64,384]{2,1,0:T(8,128)}, f32[20,64,384]{2,1,0:T(8,128)}, f32[20,64,384]{2,1,0:T(8,128)}) fusion(f32[20,68,388]{2,1,0:T(8,128)S(1)} %get-tuple-element.75), kind=kLoop, calls=%fused_computation.368 | loop fusion | bytes 19660800 | tf_op jit(solution)/shard_map/slice | solution.py:54
  209.2 8.1 %fusion.43 = (f32[20,64,384]{2,1,0:T(8,128)}, f32[20,64,384]{2,1,0:T(8,128)}) fusion(f32[20,68,388]{2,1,0:T(8,128)} %get-tuple-element.74), kind=kLoop, calls=%fused_computation.83 | loop fusion | flops 1966080 | bytes 9830400 | tf_op jit(solution)/shard_map/mul | solution.py:68
  217.3 3.6 fusion.45
  222.3 19.5 %fusion.2 = f32[2,20,66,386]{3,2,1,0:T(8,128)} fusion(f32[5,20,68,388]{3,2,1,0:T(8,128)} %copy-done, f32[5,20,2,388]{3,2,1,0:T(2,128)S(1)} %copy-done.16, f32[5,20,64,2]{3,2,1,0:T(8,128)S(1)} %copy-done.4, f32[5,20,64,2]{3,2,1,0:T(8,128)S(1)} %copy-done.5, f32[1,20,64,384]{3,2,1,0:T(8,128)S(1)} %copy-done.7, f32[1,20,64,384]{3,2,1,0:T(8,128)S(1)} %copy-done.9, ...), kind=kLoop, calls=%fused_computation.4 | loop fusion | flops 24456960 | bytes 37048640 | tf_op jit(solution)/shard_map/mul | solution.py:64
  241.9 33.9 %fusion.15 = f32[2,20,64,384]{3,2,1,0:T(8,128)} fusion(f32[2,20,66,386]{3,2,1,0:T(8,128)} %fusion.2, f32[2,20,64,384]{3,2,1,0:T(8,128)} %param.9, f32[5,20,2,388]{3,2,1,0:T(2,128)} %copy.284, f32[5,20,64,2]{3,2,1,0:T(8,128)S(1)} %copy-done.4, f32[5,20,64,2]{3,2,1,0:T(8,128)} %copy.277, f32[1,20,64,384]{3,2,1,0:T(8,128)} %copy-done.6, ...), kind=kLoop, calls=%fused_computation.31 | loop fusion | flops 55050240 | bytes 51841280 | tf_op jit(solution)/shard_map/mul | solution.py:115
  275.8 4.8 subtract_dynamic-update-slice_fusion
  287.4 11.8 %all_to_all.34 = f32[3,64,384]{2,0,1:T(4,128)S(1)} all-to-all(f32[3,64,384]{2,0,1:T(4,128)S(1)} %copy.351), channel_id=1, replica_groups=mesh['lon'=8,'lat'=16] {'lon'}, dimensions={1} | all-to-all | bytes 589824 | tf_op jit(solution)/shard_map/all_to_all | solution.py:264
  302.1 3.5 collective-permute-start.8
  309.1 3.3 collective-permute-done.10
  314.5 4.6 collective-permute-start.11
  325.0 3.9 collective-permute-done.13
  331.5 3.9 collective-permute-start.15
  338.8 2.7 collective-permute-start.17
  345.2 6.7 %collective-permute-start.18 = (f32[]{:T(128)}, f32[]{:T(128)}, u32[]{:S(2)}, u32[]{:S(2)}) collective-permute-start(f32[]{:T(128)} %get-tuple-element.10), channel_id=1, source_target_pairs={{0,16},{16,0},{32,48},{48,32},{64,80},{80,64},{96,112},{112,96},{1... | collective-permute-start | bytes 20 | tf_op jit(solution)/shard_map/ppermute | solution.py:192
  358.1 3.1 collective-permute-done.20
  365.0 4.3 collective-permute-start.22
  373.3 3.5 collective-permute-start.24
  378.5 7.2 %collective-permute-start.25 = (f32[1,3072]{1,0:T(1,128)S(1)}, f32[1,3072]{1,0:T(1,128)S(1)}, u32[]{:S(2)}, u32[]{:S(2)}) collective-permute-start(f32[1,3072]{1,0:T(1,128)S(1)} %get-tuple-element.125), channel_id=1, source_target_pairs={{0,16},{16,32},{32,48},{48,64},{64,80},{80,96},{96,112},{112,0},{1... | collective-permute-start | bytes 36872 | tf_op jit(solution)/shard_map/ppermute | solution.py:42
  386.8 3.2 collective-permute-start.26
  393.4 3.3 collective-permute-done.28
  397.7 4.9 collective-permute-start.29
  408.7 3.1 collective-permute-done.31
  415.6 4.9 collective-permute-start.33
  424.2 3.4 collective-permute-start.35
  429.3 7.6 %collective-permute-start.36 = (f32[]{:T(128)}, f32[]{:T(128)}, u32[]{:S(2)}, u32[]{:S(2)}) collective-permute-start(f32[]{:T(128)} %get-tuple-element.6), channel_id=1, source_target_pairs={{0,16},{16,0},{32,48},{48,32},{64,80},{80,64},{96,112},{112,96},{1... | collective-permute-start | bytes 20 | tf_op jit(solution)/shard_map/ppermute | solution.py:192
  443.0 3.1 collective-permute-done.38
  449.7 4.3 collective-permute-start.40
  457.8 3.4 collective-permute-start.42
  462.4 7.2 %collective-permute-start.43 = (f32[1,3072]{1,0:T(1,128)S(1)}, f32[1,3072]{1,0:T(1,128)S(1)}, u32[]{:S(2)}, u32[]{:S(2)}) collective-permute-start(f32[1,3072]{1,0:T(1,128)S(1)} %get-tuple-element.123), channel_id=1, source_target_pairs={{0,16},{16,32},{32,48},{48,64},{64,80},{80,96},{96,112},{112,0},{1... | collective-permute-start | bytes 36872 | tf_op jit(solution)/shard_map/ppermute | solution.py:42
  470.7 3.0 collective-permute-start.44
  477.2 3.4 collective-permute-done.46
  481.6 4.8 collective-permute-start.47
  492.5 3.1 collective-permute-done.49
  499.4 4.7 collective-permute-start.51
  507.9 3.4 collective-permute-start.53
  512.5 15.0 %all_to_all.35 = f32[8,8,384]{2,0,1:T(8,128)S(1)} all-to-all(f32[8,8,384]{2,0,1:T(8,128)S(1)} %bitcast.186), channel_id=1, replica_groups=mesh['lon'=8,'lat'=16] {'lon'}, dimensions={1} | all-to-all | bytes 196608 | tf_op jit(solution)/shard_map/all_to_all | solution.py:272
  (377 shorter events, 227.3 us)
Async XLA Ops:
  11.6 22.6 %collective-permute-start.1 = (f32[5,20,64,2]{2,1,3,0:T(8,128)}, f32[5,20,64,2]{2,1,3,0:T(8,128)}, u32[]{:S(2)}, u32[]{:S(2)}) collective-permute-start(f32[5,20,64,2]{2,1,3,0:T(8,128)} %copy.355), channel_id=1, source_target_pairs={{16,0},{32,16},{48,32},{64,48},{80,64},{96,80},{112,96},{0,112},{1... | collective-permute-start | bytes 153608 | tf_op jit(solution)/shard_map/ppermute | solution.py:24
  15.5 21.3 %collective-permute-start = (f32[5,20,64,2]{2,1,3,0:T(8,128)}, f32[5,20,64,2]{2,1,3,0:T(8,128)}, u32[]{:S(2)}, u32[]{:S(2)}) collective-permute-start(f32[5,20,64,2]{2,1,3,0:T(8,128)} %copy.354), channel_id=1, source_target_pairs={{0,16},{16,32},{32,48},{48,64},{64,80},{80,96},{96,112},{112,0},{1... | collective-permute-start | bytes 153608 | tf_op jit(solution)/shard_map/ppermute | solution.py:21
  44.4 4.5 collective-permute-start.3
  48.8 12.9 %collective-permute-start.4 = (f32[5,20,2,388]{3,1,2,0:T(8,128)S(1)}, f32[5,20,2,388]{3,1,2,0:T(8,128)}, u32[]{:S(2)}, u32[]{:S(2)}) collective-permute-start(f32[5,20,2,388]{3,1,2,0:T(8,128)S(1)} %collective-permute-done.3), channel_id=1, source_target_pairs={{0,32},{32,0},{16,48},{48,16},{64,96},{96,64},{80,112},{112,80},{1... | collective-permute-start | bytes 931208 | tf_op jit(solution)/shard_map/ppermute | solution.py:36
  50.7 113.4 %collective-permute-start.2 = (f32[5,20,2,388]{3,1,2,0:T(8,128)}, f32[5,20,2,388]{3,1,2,0:T(8,128)}, u32[]{:S(2)}, u32[]{:S(2)}) collective-permute-start(f32[5,20,2,388]{3,1,2,0:T(8,128)} %copy.279), channel_id=1, source_target_pairs={{0,1},{1,2},{2,3},{3,4},{4,5},{5,6},{6,7},{7,8},{8,9},{9,10},{10,1... | collective-permute-start | bytes 931208 | tf_op jit(solution)/shard_map/ppermute | solution.py:21
  56.0 116.3 %collective-permute-start.6 = (f32[5,20,2,388]{3,1,2,0:T(8,128)}, f32[5,20,2,388]{3,1,2,0:T(8,128)}, u32[]{:S(2)}, u32[]{:S(2)}) collective-permute-start(f32[5,20,2,388]{3,1,2,0:T(8,128)} %copy.282), channel_id=1, source_target_pairs={{1,0},{2,1},{3,2},{4,3},{5,4},{6,5},{7,6},{8,7},{9,8},{10,9},{11,1... | collective-permute-start | bytes 931208 | tf_op jit(solution)/shard_map/ppermute | solution.py:24
  61.7 104.5 %collective-permute-start.5 = (f32[5,20,2,388]{3,1,2,0:T(8,128)}, f32[5,20,2,388]{3,1,2,0:T(8,128)}, u32[]{:S(2)}, u32[]{:S(2)}) collective-permute-start(f32[5,20,2,388]{3,1,2,0:T(8,128)} %collective-permute-done.4), channel_id=1, source_target_pairs={{0,64},{64,0},{16,80},{80,16},{32,96},{96,32},{48,112},{112,48},{1... | collective-permute-start | bytes 931208 | tf_op jit(solution)/shard_map/ppermute | solution.py:36
  301.2 6.5 %collective-permute-start.9 = (f32[1,3072]{1,0:T(1,128)S(1)}, f32[1,3072]{1,0:T(1,128)S(1)}, u32[]{:S(2)}, u32[]{:S(2)}) collective-permute-start(f32[1,3072]{1,0:T(1,128)S(1)} %get-tuple-element.126), channel_id=1, source_target_pairs={{0,112},{16,0},{32,16},{48,32},{64,48},{80,64},{96,80},{112,96},{1... | collective-permute-start | bytes 36872 | tf_op jit(solution)/shard_map/ppermute | solution.py:42
  302.1 7.0 %collective-permute-start.8 = (f32[1,3072]{1,0:T(1,128)S(1)}, f32[1,3072]{1,0:T(1,128)S(1)}, u32[]{:S(2)}, u32[]{:S(2)}) collective-permute-start(f32[1,3072]{1,0:T(1,128)S(1)} %collective-permute-done.7), channel_id=1, source_target_pairs={{0,1},{1,2},{2,3},{3,4},{4,5},{5,6},{6,7},{7,8},{8,9},{9,10},{10,1... | collective-permute-start | bytes 36872 | tf_op jit(solution)/shard_map/ppermute | solution.py:48
  307.7 4.6 collective-permute-start.10
  314.5 5.4 %collective-permute-start.11 = (f32[2]{0:T(128)S(1)}, f32[2]{0:T(128)S(1)}, u32[]{:S(2)}, u32[]{:S(2)}) collective-permute-start(f32[2]{0:T(128)S(1)} %pad_maximum_fusion.50), channel_id=1, source_target_pairs={{0,16},{16,0},{32,48},{48,32},{64,80},{80,64},{96,112},{112,96},{1... | collective-permute-start | bytes 32 | tf_op jit(solution)/shard_map/ppermute | solution.py:192
  324.9 3.9 collective-permute-start.13
  328.9 2.6 collective-permute-start.14
  331.5 4.9 collective-permute-start.15
  338.8 3.9 collective-permute-start.17
  345.2 7.8 %collective-permute-start.18 = (f32[]{:T(128)}, f32[]{:T(128)}, u32[]{:S(2)}, u32[]{:S(2)}) collective-permute-start(f32[]{:T(128)} %get-tuple-element.10), channel_id=1, source_target_pairs={{0,16},{16,0},{32,48},{48,32},{64,80},{80,64},{96,112},{112,96},{1... | collective-permute-start | bytes 20 | tf_op jit(solution)/shard_map/ppermute | solution.py:192
  354.2 2.5 collective-permute-start.19
  357.3 4.0 collective-permute-start.20
  361.9 2.5 collective-permute-start.21
  365.0 4.5 collective-permute-start.22
  370.2 2.5 collective-permute-start.23
  373.3 4.0 collective-permute-start.24
  378.5 8.3 %collective-permute-start.25 = (f32[1,3072]{1,0:T(1,128)S(1)}, f32[1,3072]{1,0:T(1,128)S(1)}, u32[]{:S(2)}, u32[]{:S(2)}) collective-permute-start(f32[1,3072]{1,0:T(1,128)S(1)} %get-tuple-element.125), channel_id=1, source_target_pairs={{0,16},{16,32},{32,48},{48,64},{64,80},{80,96},{96,112},{112,0},{1... | collective-permute-start | bytes 36872 | tf_op jit(solution)/shard_map/ppermute | solution.py:42
  385.7 6.4 %collective-permute-start.27 = (f32[1,3072]{1,0:T(1,128)S(1)}, f32[1,3072]{1,0:T(1,128)S(1)}, u32[]{:S(2)}, u32[]{:S(2)}) collective-permute-start(f32[1,3072]{1,0:T(1,128)S(1)} %get-tuple-element.124), channel_id=1, source_target_pairs={{0,112},{16,0},{32,16},{48,32},{64,48},{80,64},{96,80},{112,96},{1... | collective-permute-start | bytes 36872 | tf_op jit(solution)/shard_map/ppermute | solution.py:42
  386.8 6.6 %collective-permute-start.26 = (f32[1,3072]{1,0:T(1,128)S(1)}, f32[1,3072]{1,0:T(1,128)S(1)}, u32[]{:S(2)}, u32[]{:S(2)}) collective-permute-start(f32[1,3072]{1,0:T(1,128)S(1)} %collective-permute-done.25), channel_id=1, source_target_pairs={{0,1},{1,2},{2,3},{3,4},{4,5},{5,6},{6,7},{7,8},{8,9},{9,10},{10,1... | collective-permute-start | bytes 36872 | tf_op jit(solution)/shard_map/ppermute | solution.py:48
  392.1 4.6 collective-permute-start.28
  397.7 6.0 %collective-permute-start.29 = (f32[]{:T(128)}, f32[]{:T(128)}, u32[]{:S(2)}, u32[]{:S(2)}) collective-permute-start(f32[]{:T(128)} %get-tuple-element.8), channel_id=1, source_target_pairs={{0,16},{16,0},{32,48},{48,32},{64,80},{80,64},{96,112},{112,96},{1... | collective-permute-start | bytes 20 | tf_op jit(solution)/shard_map/ppermute | solution.py:192
  404.8 2.5 collective-permute-start.30
  407.8 4.0 collective-permute-start.31
  412.4 2.6 collective-permute-start.32
  415.6 5.0 collective-permute-start.33
  424.2 4.0 collective-permute-start.35
  429.3 8.7 %collective-permute-start.36 = (f32[]{:T(128)}, f32[]{:T(128)}, u32[]{:S(2)}, u32[]{:S(2)}) collective-permute-start(f32[]{:T(128)} %get-tuple-element.6), channel_id=1, source_target_pairs={{0,16},{16,0},{32,48},{48,32},{64,80},{80,64},{96,112},{112,96},{1... | collective-permute-start | bytes 20 | tf_op jit(solution)/shard_map/ppermute | solution.py:192
  439.2 2.5 collective-permute-start.37
  442.2 4.0 collective-permute-start.38
  446.7 2.5 collective-permute-start.39
  449.7 4.5 collective-permute-start.40
  457.8 4.0 collective-permute-start.42
  462.4 8.3 %collective-permute-start.43 = (f32[1,3072]{1,0:T(1,128)S(1)}, f32[1,3072]{1,0:T(1,128)S(1)}, u32[]{:S(2)}, u32[]{:S(2)}) collective-permute-start(f32[1,3072]{1,0:T(1,128)S(1)} %get-tuple-element.123), channel_id=1, source_target_pairs={{0,16},{16,32},{32,48},{48,64},{64,80},{80,96},{96,112},{112,0},{1... | collective-permute-start | bytes 36872 | tf_op jit(solution)/shard_map/ppermute | solution.py:42
  469.6 6.2 %collective-permute-start.45 = (f32[1,3072]{1,0:T(1,128)S(1)}, f32[1,3072]{1,0:T(1,128)S(1)}, u32[]{:S(2)}, u32[]{:S(2)}) collective-permute-start(f32[1,3072]{1,0:T(1,128)S(1)} %get-tuple-element.122), channel_id=1, source_target_pairs={{0,112},{16,0},{32,16},{48,32},{64,48},{80,64},{96,80},{112,96},{1... | collective-permute-start | bytes 36872 | tf_op jit(solution)/shard_map/ppermute | solution.py:42
  470.7 6.4 %collective-permute-start.44 = (f32[1,3072]{1,0:T(1,128)S(1)}, f32[1,3072]{1,0:T(1,128)S(1)}, u32[]{:S(2)}, u32[]{:S(2)}) collective-permute-start(f32[1,3072]{1,0:T(1,128)S(1)} %collective-permute-done.43), channel_id=1, source_target_pairs={{0,1},{1,2},{2,3},{3,4},{4,5},{5,6},{6,7},{7,8},{8,9},{9,10},{10,1... | collective-permute-start | bytes 36872 | tf_op jit(solution)/shard_map/ppermute | solution.py:48
  475.8 4.8 collective-permute-start.46
  481.6 5.9 %collective-permute-start.47 = (f32[]{:T(128)}, f32[]{:T(128)}, u32[]{:S(2)}, u32[]{:S(2)}) collective-permute-start(f32[]{:T(128)} %fusion.97), channel_id=1, source_target_pairs={{0,16},{16,0},{32,48},{48,32},{64,80},{80,64},{96,112},{112,96},{1... | collective-permute-start | bytes 20 | tf_op jit(solution)/shard_map/ppermute | solution.py:192
  488.7 2.5 collective-permute-start.48
  491.7 4.0 collective-permute-start.49
  496.2 2.7 collective-permute-start.50
  499.4 4.9 collective-permute-start.51
  507.9 4.0 collective-permute-start.53
  (77 other events, 621.7 us)

commit v2 on v1

--- a/solution.py
+++ b/solution.py
@@ -2,6 +2,8 @@
 import jax.numpy as jnp
 from jax import lax
 from jax.sharding import PartitionSpec as P
+from jax.experimental import pallas as pl
+from jax.experimental.pallas import tpu as pltpu
 
 ITERS = 3
 
@@ -115,30 +117,61 @@
     return wet_centre * (centre - advection_rate * divergence - biharmonic_rate * lap_two)
 
 
+def mix_kernel(values_ref, wet_ref, diff_ref, out_ref, ratio_ref):
+    level_count = wet_ref.shape[0]
+    tracer_count = values_ref.shape[0]
+
+    def coupling(k):
+        return diff_ref[k].astype(jnp.float32) * wet_ref[k] * wet_ref[k - 1]
+
+    below = coupling(1)
+    upper = None
+    reduced = [None] * tracer_count
+    for k in range(level_count):
+        above = below
+        below = coupling(k + 1) if k + 1 < level_count else None
+        if k == 0:
+            diagonal = 1.0 + below
+            divisor = diagonal
+        elif below is None:
+            diagonal = 1.0 + above
+            divisor = diagonal + above * upper
+        else:
+            diagonal = 1.0 + above + below
+            divisor = diagonal + above * upper
+        if below is not None:
+            upper = -below / divisor
+            ratio_ref[k] = upper
+        for t in range(tracer_count):
+            if k == 0:
+                source = values_ref[t, 0]
+            else:
+                source = values_ref[t, k] + above * reduced[t]
+            reduced[t] = source / divisor
+            out_ref[t, k] = reduced[t]
+    result = reduced
+    for k in range(level_count - 2, -1, -1):
+        ratio = ratio_ref[k]
+        for t in range(tracer_count):
+            result[t] = out_ref[t, k] - ratio * result[t]
+            out_ref[t, k] = result[t]
+
+
 def vertical_mix(values, wet_mask, diffusivity):
-    level_count = wet_mask.shape[0]
-    zeros_plane = jnp.zeros_like(wet_mask[0])
-    coupling = (
-        [zeros_plane]
-        + [diffusivity[k] * wet_mask[k] * wet_mask[k - 1] for k in range(1, level_count)]
-        + [zeros_plane]
-    )
-    upper_ratio = []
-    reduced = []
-    for k in range(level_count):
-        diagonal = 1.0 + coupling[k] + coupling[k + 1]
-        if k == 0:
-            divisor = diagonal
-            source = values[:, 0]
-        else:
-            divisor = diagonal + coupling[k] * upper_ratio[k - 1]
-            source = values[:, k] + coupling[k] * reduced[k - 1]
-        upper_ratio.append(-coupling[k + 1] / divisor)
-        reduced.append(source / divisor)
-    result = [reduced[-1]]
-    for k in range(level_count - 2, -1, -1):
-        result.insert(0, reduced[k] - upper_ratio[k] * result[0])
-    return jnp.stack(result, axis=1)
+    tracer_count, level_count, row_count, col_count = values.shape
+    rows = 16 if row_count % 16 == 0 else row_count
+    return pl.pallas_call(
+        mix_kernel,
+        grid=(row_count // rows,),
+        in_specs=[
+            pl.BlockSpec((tracer_count, level_count, rows, col_count), lambda i: (0, 0, i, 0)),
+            pl.BlockSpec((level_count, rows, col_count), lambda i: (0, i, 0)),
+            pl.BlockSpec((level_count, rows, col_count), lambda i: (0, i, 0)),
+        ],
+        out_specs=pl.BlockSpec((tracer_count, level_count, rows, col_count), lambda i: (0, 0, i, 0)),
+        out_shape=jax.ShapeDtypeStruct(values.shape, jnp.float32),
+        scratch_shapes=[pltpu.VMEM((level_count - 1, rows, col_count), jnp.float32)],
+    )(values, wet_mask, diffusivity)
 
 
 def nine_point(padded, wet_surface, centre_weight):
@@ -257,7 +290,7 @@
     fold_signs = jnp.array([1.0, 1.0, 1.0, -1.0, -1.0], jnp.float32).reshape(5, 1, 1, 1)
     padded = clinic_extend(stacked, fold_signs)
     provisional = baroclinic(padded)
-    new_tracers = vertical_mix(provisional, wet_mask, vertical_diffusivity.astype(jnp.float32))
+    new_tracers = vertical_mix(provisional, wet_mask, vertical_diffusivity)
     wet_surface = wet_mask[0]
     surface_source = wet_surface * (forcing + jnp.mean(new_tracers[0] - new_tracers[1], axis=0))
     centre_weight = 6.0 + surface_coupling

time: 538 us -> 419 us (0.78)
  local copies, waits for them, and re-layouts: 159 us -> 45.9 us
  other arithmetic: 127 us -> 103 us
  waiting for transfers between devices: 57.6 us -> 69.5 us
  Pallas kernels: 0 us -> 5.69 us
    mul x38 -> x0, local copies, waits for them, and re-layouts: 64 us -> none  [the longest x19 32 us: vertical_mix(): source = values[:, k] + coupling[k] * reduced[k - 1]]
    div x20 -> x0, local copies, waits for them, and re-layouts: 31.9 us -> none  [vertical_mix(): reduced.append(source / divisor)]
    unnamed x163 -> x43, local copies, waits for them, and re-layouts: 24.9 us -> 9.31 us
    mul x11 -> x0, other arithmetic: 10.4 us -> none  [vertical_mix(): result.insert(0, reduced[k] - upper_ratio[k] * result[0])]
    ppermute x3, waiting for transfers between devices: 4.45 us -> 13.9 us  [from_partner(): return lax.ppermute(block, axis, route)]
    unnamed x10 -> x0, other arithmetic: 6.14 us -> none
    div x5 -> x0, other arithmetic: 6.11 us -> none  [vertical_mix(): reduced.append(source / divisor)]
    pallas_call x0 -> x1, Pallas kernels: none -> 5.69 us  [vertical_mix(): pl.pallas_call(mix_kernel, grid=(row_count // rows,), in_specs=[pl.BlockS...]
  transfers between devices with their start and end apart: 54 -> 54, of which waited for: 42 -> 46; matrix products, arithmetic and copies ran while one was open for 27% -> 4% of each run, Pallas kernels for 0% -> 0%
where the time goes in v2:
time: 419 us; the launch traced here: 412 us
  starting transfers between devices  135 us (32%)
  other arithmetic  103 us (25%)
  waiting for transfers between devices  69.5 us (17%)
  local copies, waits for them, and re-layouts  45.9 us (11%)
  blocking collectives  28.8 us (7%)
  between operations  23.7 us (6%)
  Pallas kernels  5.69 us (1%)
    ppermute x35, starting transfers between devices, butterfly_sum(): lax.ppermute(value, axis, [(i, i ^ bit) for i in range(count)])  93.4 us
    ppermute x35, waiting for transfers between devices, butterfly_sum(): lax.ppermute(value, axis, [(i, i ^ bit) for i in range(count)])  41 us
    mul x1, other arithmetic, baroclinic(): wet_centre * (centre - advection_rate * divergence - biharmonic_rate * la...  32.5 us
    mul x1, other arithmetic, masked_laplacian(): return window(wet_mask, 1, 1) * running  20.3 us
    ppermute x6, starting transfers between devices, passed_along(): return lax.ppermute(value, axis, pairs)  16.3 us
    all_to_all x1, blocking collectives, shards(): lax.all_to_all(strip_solution, 'lon', split_axis=1, concat_axis=0, tiled=...  15 us
    ppermute x3, waiting for transfers between devices, from_partner(): return lax.ppermute(block, axis, route)  13.9 us
    all_to_all x1, blocking collectives, shards(): lax.all_to_all(jnp.stack([surface_source, wet_surface, centre_weight]), '...  13.8 us
  transfers between devices with their start and end apart: 54, of which 46 were waited for; matrix products, arithmetic and copies ran while one was open for 4% of the time, Pallas kernels for 0%

profile of v2, /device:TPU:1, one launch (start us, length us, event | category | flops | bytes accessed | tf_op | source)
XLA Modules:
  0.0 411.8 jit_solution(14606535199596296565)
XLA Ops:
  4.3 3.4 pad_maximum_fusion.24
  7.8 3.2 copy.24
  19.8 3.1 copy.27
  23.0 3.9 pad_maximum_fusion.30
  31.4 8.5 %collective-permute-done.4 = f32[5,20,2,388]{3,2,1,0:T(2,128)} collective-permute-done((f32[5,20,2,388]{3,2,1,0:T(2,128)S(1)}, f32[5,20,2,388]{3,2,1,0:T(2,128)}, u32[]{:S(2)}, u32[]{:S(2)}) %collective-permute-start.4) | collective-permute-done | bytes 310432 | tf_op jit(solution)/shard_map/ppermute | solution.py:38
  43.8 4.3 %collective-permute-start.2 = (f32[5,20,2,388]{3,2,1,0:T(2,128)}, f32[5,20,2,388]{3,2,1,0:T(2,128)}, u32[]{:S(2)}, u32[]{:S(2)}) collective-permute-start(f32[5,20,2,388]{3,2,1,0:T(2,128)} %get-tuple-element.10), channel_id=1, source_target_pairs={{0,1},{1,2},{2,3},{3,4},{4,5},{5,6},{6,7},{7,8},{8,9},{9,10},{10,1... | collective-permute-start | bytes 931208 | tf_op jit(solution)/shard_map/ppermute | solution.py:23
  48.2 3.5 collective-permute-done.5
  51.7 3.8 reverse
  57.2 13.5 %pad_maximum_fusion = f32[5,20,68,388]{3,2,1,0:T(8,128)S(1)} fusion(f32[5,20,2,388]{3,2,1,0:T(2,128)S(1)} %multiply_select_fusion, f32[5,20,64,2]{3,2,1,0:T(8,128)} %copy.27, f32[1,20,64,384]{3,2,1,0:T(8,128)} %copy-done.6, f32[1,20,64,384]{3,2,1,0:T(8,128)} %copy-done.8, f32[1,20,64,384]{3,2,1,0:T(8,128)} %copy-done.10, f32[2,20,64,384]{3,2,1,0:T(8,128)} %param.9, ...), kind=kLoop, calls=%fused_computation | loop fusion | flops 18468800 | bytes 21107200 | tf_op jit(solution)/shard_map/concatenate | solution.py:198
  70.7 4.0 slice_bitcast_fusion.1
  74.7 2.9 copy-done
  77.7 8.4 %fusion.74 = (f32[20,66,386]{2,1,0:T(8,128)}, f32[20,66,386]{2,1,0:T(8,128)}, f32[20,66,386]{2,1,0:T(8,128)}, f32[20,66,386]{2,1,0:T(8,128)}, f32[20,66,386]{2,1,0:T(8,128)}) fusion(f32[20,68,388]{2,1,0:T(8,128)S(1)} %get-tuple-element.14), kind=kLoop, calls=%fused_computation.187 | loop fusion | bytes 20380800 | tf_op jit(solution)/shard_map/slice | solution.py:77
  86.1 6.4 %fusion.73 = (f32[20,64,384]{2,1,0:T(8,128)}, f32[20,64,384]{2,1,0:T(8,128)}, f32[20,64,384]{2,1,0:T(8,128)}, f32[20,64,384]{2,1,0:T(8,128)}, f32[20,64,384]{2,1,0:T(8,128)}) fusion(f32[20,68,388]{2,1,0:T(8,128)S(1)} %get-tuple-element.14), kind=kLoop, calls=%fused_computation.186 | loop fusion | bytes 19660800 | tf_op jit(solution)/shard_map/slice | solution.py:56
  92.4 7.8 %fusion.44 = (f32[20,64,384]{2,1,0:T(8,128)}, f32[20,64,384]{2,1,0:T(8,128)}) fusion(f32[20,68,388]{2,1,0:T(8,128)} %get-tuple-element.12), kind=kLoop, calls=%fused_computation.85 | loop fusion | flops 1966080 | bytes 9830400 | tf_op jit(solution)/shard_map/mul | solution.py:70
  100.2 3.8 fusion.42
  105.3 20.3 %fusion.2 = f32[2,20,66,386]{3,2,1,0:T(8,128)} fusion(f32[5,20,68,388]{3,2,1,0:T(8,128)} %copy-done, f32[5,20,2,388]{3,2,1,0:T(2,128)S(1)} %copy-done.14, f32[5,20,64,2]{3,2,1,0:T(8,128)S(1)} %copy-done.5, f32[5,20,64,2]{3,2,1,0:T(8,128)S(1)} %copy-done.4, f32[1,20,64,384]{3,2,1,0:T(8,128)S(1)} %copy-done.7, f32[1,20,64,384]{3,2,1,0:T(8,128)S(1)} %copy-done.9, ...), kind=kLoop, calls=%fused_computation.4 | loop fusion | flops 24456960 | bytes 37048640 | tf_op jit(solution)/shard_map/mul | solution.py:66
  125.6 32.5 %fusion.15.values_ref = f32[2,20,64,384]{3,2,1,0:T(8,128)} fusion(f32[2,20,66,386]{3,2,1,0:T(8,128)} %fusion.2, f32[2,20,64,384]{3,2,1,0:T(8,128)} %param.9, f32[5,20,2,388]{3,2,1,0:T(2,128)} %collective-permute-done.2, f32[5,20,64,2]{3,2,1,0:T(8,128)} %copy.27, f32[5,20,64,2]{3,2,1,0:T(8,128)S(1)} %copy-done.4, f32[1,20,64,384]{3,2,1,0:T(8,128)} %copy-done.6, ...), kind=kLoop, calls=%fused_computation.31 | loop fusion | flops 55050240 | bytes 51841280 | tf_op jit(solution)/shard_map/mul | solution.py:117
  158.1 5.7 %shard_map.104 = f32[2,20,64,384]{3,2,1,0:T(8,128)} custom-call(f32[2,20,64,384]{3,2,1,0:T(8,128)} %fusion.15.values_ref, f32[20,64,384]{2,1,0:T(8,128)} %fusion.46.wet_ref, bf16[20,64,384]{2,1,0:T(8,128)(2,1)} %diff_ref.1), custom_call_target="tpu_custom_call" | custom-call | tf_op jit(solution)/shard_map/pallas_call | solution.py:163
  166.8 13.8 %all_to_all.34 = f32[3,64,384]{2,0,1:T(4,128)S(1)} all-to-all(f32[3,64,384]{2,0,1:T(4,128)S(1)} %copy.30), channel_id=1, replica_groups=mesh['lon'=8,'lat'=16] {'lon'}, dimensions={1} | all-to-all | bytes 589824 | tf_op jit(solution)/shard_map/all_to_all | solution.py:297
  183.4 3.6 collective-permute-start.8
  190.5 3.3 collective-permute-done.10
  196.1 4.6 %collective-permute-start.11 = (f32[2]{0:T(128)S(1)}, f32[2]{0:T(128)S(1)}, u32[]{:S(2)}, u32[]{:S(2)}) collective-permute-start(f32[2]{0:T(128)S(1)} %pad_maximum_fusion.50), channel_id=1, source_target_pairs={{0,16},{16,0},{32,48},{48,32},{64,80},{80,64},{96,112},{112,96},{1... | collective-permute-start | bytes 32 | tf_op jit(solution)/shard_map/ppermute | solution.py:225
  206.7 3.9 collective-permute-done.13
  213.3 3.7 collective-permute-start.15
  220.3 2.7 collective-permute-start.17
  226.8 6.7 %collective-permute-start.18 = (f32[]{:T(128)}, f32[]{:T(128)}, u32[]{:S(2)}, u32[]{:S(2)}) collective-permute-start(f32[]{:T(128)} %get-tuple-element.6), channel_id=1, source_target_pairs={{0,16},{16,0},{32,48},{48,32},{64,80},{80,64},{96,112},{112,96},{1... | collective-permute-start | bytes 20 | tf_op jit(solution)/shard_map/ppermute | solution.py:225
  239.9 3.1 collective-permute-done.20
  246.6 4.3 %collective-permute-start.22 = (f32[]{:T(128)}, f32[]{:T(128)}, u32[]{:S(2)}, u32[]{:S(2)}) collective-permute-start(f32[]{:T(128)} %add.259), channel_id=1, source_target_pairs={{0,2},{1,3},{2,0},{3,1},{4,6},{5,7},{6,4},{7,5},{8,10},{9,11},{10,... | collective-permute-start | bytes 20 | tf_op jit(solution)/shard_map/ppermute | solution.py:225
  254.7 3.5 collective-permute-start.24
  260.0 7.2 %collective-permute-start.25 = (f32[1,3072]{1,0:T(1,128)S(1)}, f32[1,3072]{1,0:T(1,128)S(1)}, u32[]{:S(2)}, u32[]{:S(2)}) collective-permute-start(f32[1,3072]{1,0:T(1,128)S(1)} %get-tuple-element.44), channel_id=1, source_target_pairs={{0,16},{16,32},{32,48},{48,64},{64,80},{80,96},{96,112},{112,0},{1... | collective-permute-start | bytes 36872 | tf_op jit(solution)/shard_map/ppermute | solution.py:44
  268.3 3.2 collective-permute-start.26
  274.9 3.3 collective-permute-done.28
  279.2 4.9 %collective-permute-start.29 = (f32[]{:T(128)}, f32[]{:T(128)}, u32[]{:S(2)}, u32[]{:S(2)}) collective-permute-start(f32[]{:T(128)} %get-tuple-element.4), channel_id=1, source_target_pairs={{0,16},{16,0},{32,48},{48,32},{64,80},{80,64},{96,112},{112,96},{1... | collective-permute-start | bytes 20 | tf_op jit(solution)/shard_map/ppermute | solution.py:225
  290.3 3.1 collective-permute-done.31
  297.4 4.9 %collective-permute-start.33 = (f32[]{:T(128)}, f32[]{:T(128)}, u32[]{:S(2)}, u32[]{:S(2)}) collective-permute-start(f32[]{:T(128)} %add.273), channel_id=1, source_target_pairs={{0,2},{1,3},{2,0},{3,1},{4,6},{5,7},{6,4},{7,5},{8,10},{9,11},{10,... | collective-permute-start | bytes 20 | tf_op jit(solution)/shard_map/ppermute | solution.py:225
  306.2 3.4 collective-permute-start.35
  311.4 7.6 %collective-permute-start.36 = (f32[]{:T(128)}, f32[]{:T(128)}, u32[]{:S(2)}, u32[]{:S(2)}) collective-permute-start(f32[]{:T(128)} %get-tuple-element.2), channel_id=1, source_target_pairs={{0,16},{16,0},{32,48},{48,32},{64,80},{80,64},{96,112},{112,96},{1... | collective-permute-start | bytes 20 | tf_op jit(solution)/shard_map/ppermute | solution.py:225
  325.3 3.1 collective-permute-done.38
  332.2 4.3 %collective-permute-start.40 = (f32[]{:T(128)}, f32[]{:T(128)}, u32[]{:S(2)}, u32[]{:S(2)}) collective-permute-start(f32[]{:T(128)} %add.281), channel_id=1, source_target_pairs={{0,2},{1,3},{2,0},{3,1},{4,6},{5,7},{6,4},{7,5},{8,10},{9,11},{10,... | collective-permute-start | bytes 20 | tf_op jit(solution)/shard_map/ppermute | solution.py:225
  340.4 3.4 collective-permute-start.42
  345.1 7.2 %collective-permute-start.43 = (f32[1,3072]{1,0:T(1,128)S(1)}, f32[1,3072]{1,0:T(1,128)S(1)}, u32[]{:S(2)}, u32[]{:S(2)}) collective-permute-start(f32[1,3072]{1,0:T(1,128)S(1)} %get-tuple-element.42), channel_id=1, source_target_pairs={{0,16},{16,32},{32,48},{48,64},{64,80},{80,96},{96,112},{112,0},{1... | collective-permute-start | bytes 36872 | tf_op jit(solution)/shard_map/ppermute | solution.py:44
  353.4 3.0 collective-permute-start.44
  359.9 3.4 collective-permute-done.46
  364.3 4.8 %collective-permute-start.47 = (f32[]{:T(128)}, f32[]{:T(128)}, u32[]{:S(2)}, u32[]{:S(2)}) collective-permute-start(f32[]{:T(128)} %fusion.57), channel_id=1, source_target_pairs={{0,16},{16,0},{32,48},{48,32},{64,80},{80,64},{96,112},{112,96},{1... | collective-permute-start | bytes 20 | tf_op jit(solution)/shard_map/ppermute | solution.py:225
  375.3 3.1 collective-permute-done.49
  382.5 4.7 %collective-permute-start.51 = (f32[]{:T(128)}, f32[]{:T(128)}, u32[]{:S(2)}, u32[]{:S(2)}) collective-permute-start(f32[]{:T(128)} %add.295), channel_id=1, source_target_pairs={{0,2},{1,3},{2,0},{3,1},{4,6},{5,7},{6,4},{7,5},{8,10},{9,11},{10,... | collective-permute-start | bytes 20 | tf_op jit(solution)/shard_map/ppermute | solution.py:225
  391.1 3.4 collective-permute-start.53
  395.8 15.0 %all_to_all.35 = f32[8,8,384]{2,0,1:T(8,128)S(1)} all-to-all(f32[8,8,384]{2,0,1:T(8,128)S(1)} %bitcast.65), channel_id=1, replica_groups=mesh['lon'=8,'lat'=16] {'lon'}, dimensions={1} | all-to-all | bytes 196608 | tf_op jit(solution)/shard_map/all_to_all | solution.py:305
  (170 shorter events, 102.7 us)
Async XLA Ops:
  10.9 4.6 %collective-permute-start = (f32[5,20,64,2]{2,3,1,0:T(2,128)}, f32[5,20,64,2]{2,3,1,0:T(2,128)}, u32[]{:S(2)}, u32[]{:S(2)}) collective-permute-start(f32[5,20,64,2]{2,3,1,0:T(2,128)} %copy.24), channel_id=1, source_target_pairs={{0,16},{16,32},{32,48},{48,64},{64,80},{80,96},{96,112},{112,0},{1... | collective-permute-start | bytes 153608 | tf_op jit(solution)/shard_map/ppermute | solution.py:23
  15.4 4.4 %collective-permute-start.1 = (f32[5,20,64,2]{2,3,1,0:T(2,128)}, f32[5,20,64,2]{2,3,1,0:T(2,128)}, u32[]{:S(2)}, u32[]{:S(2)}) collective-permute-start(f32[5,20,64,2]{2,3,1,0:T(2,128)} %copy.25), channel_id=1, source_target_pairs={{16,0},{32,16},{48,32},{64,48},{80,64},{96,80},{112,96},{0,112},{1... | collective-permute-start | bytes 153608 | tf_op jit(solution)/shard_map/ppermute | solution.py:26
  28.9 11.0 %collective-permute-start.4 = (f32[5,20,2,388]{3,2,1,0:T(2,128)S(1)}, f32[5,20,2,388]{3,2,1,0:T(2,128)}, u32[]{:S(2)}, u32[]{:S(2)}) collective-permute-start(f32[5,20,2,388]{3,2,1,0:T(2,128)S(1)} %collective-permute-done.3), channel_id=1, source_target_pairs={{0,32},{32,0},{16,48},{48,16},{64,96},{96,64},{80,112},{112,80},{1... | collective-permute-start | bytes 931208 | tf_op jit(solution)/shard_map/ppermute | solution.py:38
  30.1 25.5 %collective-permute-start.6 = (f32[5,20,2,388]{3,2,1,0:T(2,128)}, f32[5,20,2,388]{3,2,1,0:T(2,128)}, u32[]{:S(2)}, u32[]{:S(2)}) collective-permute-start(f32[5,20,2,388]{3,2,1,0:T(2,128)} %get-tuple-element.11), channel_id=1, source_target_pairs={{1,0},{2,1},{3,2},{4,3},{5,4},{6,5},{7,6},{8,7},{9,8},{10,9},{11,1... | collective-permute-start | bytes 931208 | tf_op jit(solution)/shard_map/ppermute | solution.py:26
  39.9 11.9 %collective-permute-start.5 = (f32[5,20,2,388]{3,2,1,0:T(2,128)}, f32[5,20,2,388]{3,2,1,0:T(2,128)}, u32[]{:S(2)}, u32[]{:S(2)}) collective-permute-start(f32[5,20,2,388]{3,2,1,0:T(2,128)} %collective-permute-done.4), channel_id=1, source_target_pairs={{0,64},{64,0},{16,80},{80,16},{32,96},{96,32},{48,112},{112,48},{1... | collective-permute-start | bytes 931208 | tf_op jit(solution)/shard_map/ppermute | solution.py:38
  43.8 13.4 %collective-permute-start.2 = (f32[5,20,2,388]{3,2,1,0:T(2,128)}, f32[5,20,2,388]{3,2,1,0:T(2,128)}, u32[]{:S(2)}, u32[]{:S(2)}) collective-permute-start(f32[5,20,2,388]{3,2,1,0:T(2,128)} %get-tuple-element.10), channel_id=1, source_target_pairs={{0,1},{1,2},{2,3},{3,4},{4,5},{5,6},{6,7},{7,8},{8,9},{9,10},{10,1... | collective-permute-start | bytes 931208 | tf_op jit(solution)/shard_map/ppermute | solution.py:23
  182.6 6.6 %collective-permute-start.9 = (f32[1,3072]{1,0:T(1,128)S(1)}, f32[1,3072]{1,0:T(1,128)S(1)}, u32[]{:S(2)}, u32[]{:S(2)}) collective-permute-start(f32[1,3072]{1,0:T(1,128)S(1)} %get-tuple-element.45), channel_id=1, source_target_pairs={{0,112},{16,0},{32,16},{48,32},{64,48},{80,64},{96,80},{112,96},{1... | collective-permute-start | bytes 36872 | tf_op jit(solution)/shard_map/ppermute | solution.py:44
  183.4 7.1 %collective-permute-start.8 = (f32[1,3072]{1,0:T(1,128)S(1)}, f32[1,3072]{1,0:T(1,128)S(1)}, u32[]{:S(2)}, u32[]{:S(2)}) collective-permute-start(f32[1,3072]{1,0:T(1,128)S(1)} %collective-permute-done.7), channel_id=1, source_target_pairs={{0,1},{1,2},{2,3},{3,4},{4,5},{5,6},{6,7},{7,8},{8,9},{9,10},{10,1... | collective-permute-start | bytes 36872 | tf_op jit(solution)/shard_map/ppermute | solution.py:50
  189.2 4.6 %collective-permute-start.10 = (f32[1,3072]{1,0:T(1,128)S(1)}, f32[1,3072]{1,0:T(1,128)S(1)}, u32[]{:S(2)}, u32[]{:S(2)}) collective-permute-start(f32[1,3072]{1,0:T(1,128)S(1)} %collective-permute-done.9), channel_id=1, source_target_pairs={{1,0},{2,1},{3,2},{4,3},{5,4},{6,5},{7,6},{8,7},{9,8},{10,9},{11,1... | collective-permute-start | bytes 36872 | tf_op jit(solution)/shard_map/ppermute | solution.py:50
  196.1 5.4 %collective-permute-start.11 = (f32[2]{0:T(128)S(1)}, f32[2]{0:T(128)S(1)}, u32[]{:S(2)}, u32[]{:S(2)}) collective-permute-start(f32[2]{0:T(128)S(1)} %pad_maximum_fusion.50), channel_id=1, source_target_pairs={{0,16},{16,0},{32,48},{48,32},{64,80},{80,64},{96,112},{112,96},{1... | collective-permute-start | bytes 32 | tf_op jit(solution)/shard_map/ppermute | solution.py:225
  206.7 3.9 collective-permute-start.13
  210.7 2.6 collective-permute-start.14
  213.3 4.7 %collective-permute-start.15 = (f32[2]{0:T(128)S(1)}, f32[2]{0:T(128)S(1)}, u32[]{:S(2)}, u32[]{:S(2)}) collective-permute-start(f32[2]{0:T(128)S(1)} %add.252), channel_id=1, source_target_pairs={{0,2},{1,3},{2,0},{3,1},{4,6},{5,7},{6,4},{7,5},{8,10},{9,11},{10,... | collective-permute-start | bytes 32 | tf_op jit(solution)/shard_map/ppermute | solution.py:225
  220.3 3.9 collective-permute-start.17
  226.8 7.8 %collective-permute-start.18 = (f32[]{:T(128)}, f32[]{:T(128)}, u32[]{:S(2)}, u32[]{:S(2)}) collective-permute-start(f32[]{:T(128)} %get-tuple-element.6), channel_id=1, source_target_pairs={{0,16},{16,0},{32,48},{48,32},{64,80},{80,64},{96,112},{112,96},{1... | collective-permute-start | bytes 20 | tf_op jit(solution)/shard_map/ppermute | solution.py:225
  235.8 2.5 collective-permute-start.19
  238.8 4.2 %collective-permute-start.20 = (f32[]{:T(128)}, f32[]{:T(128)}, u32[]{:S(2)}, u32[]{:S(2)}) collective-permute-start(f32[]{:T(128)} %add.257), channel_id=1, source_target_pairs={{0,64},{16,80},{32,96},{48,112},{64,0},{80,16},{96,32},{112,48},{1... | collective-permute-start | bytes 20 | tf_op jit(solution)/shard_map/ppermute | solution.py:225
  243.6 2.5 collective-permute-start.21
  246.6 4.5 %collective-permute-start.22 = (f32[]{:T(128)}, f32[]{:T(128)}, u32[]{:S(2)}, u32[]{:S(2)}) collective-permute-start(f32[]{:T(128)} %add.259), channel_id=1, source_target_pairs={{0,2},{1,3},{2,0},{3,1},{4,6},{5,7},{6,4},{7,5},{8,10},{9,11},{10,... | collective-permute-start | bytes 20 | tf_op jit(solution)/shard_map/ppermute | solution.py:225
  251.7 2.5 collective-permute-start.23
  254.7 4.0 collective-permute-start.24
  260.0 8.3 %collective-permute-start.25 = (f32[1,3072]{1,0:T(1,128)S(1)}, f32[1,3072]{1,0:T(1,128)S(1)}, u32[]{:S(2)}, u32[]{:S(2)}) collective-permute-start(f32[1,3072]{1,0:T(1,128)S(1)} %get-tuple-element.44), channel_id=1, source_target_pairs={{0,16},{16,32},{32,48},{48,64},{64,80},{80,96},{96,112},{112,0},{1... | collective-permute-start | bytes 36872 | tf_op jit(solution)/shard_map/ppermute | solution.py:44
  267.2 6.4 %collective-permute-start.27 = (f32[1,3072]{1,0:T(1,128)S(1)}, f32[1,3072]{1,0:T(1,128)S(1)}, u32[]{:S(2)}, u32[]{:S(2)}) collective-permute-start(f32[1,3072]{1,0:T(1,128)S(1)} %get-tuple-element.43), channel_id=1, source_target_pairs={{0,112},{16,0},{32,16},{48,32},{64,48},{80,64},{96,80},{112,96},{1... | collective-permute-start | bytes 36872 | tf_op jit(solution)/shard_map/ppermute | solution.py:44
  268.3 6.6 %collective-permute-start.26 = (f32[1,3072]{1,0:T(1,128)S(1)}, f32[1,3072]{1,0:T(1,128)S(1)}, u32[]{:S(2)}, u32[]{:S(2)}) collective-permute-start(f32[1,3072]{1,0:T(1,128)S(1)} %collective-permute-done.25), channel_id=1, source_target_pairs={{0,1},{1,2},{2,3},{3,4},{4,5},{5,6},{6,7},{7,8},{8,9},{9,10},{10,1... | collective-permute-start | bytes 36872 | tf_op jit(solution)/shard_map/ppermute | solution.py:50
  273.6 4.6 %collective-permute-start.28 = (f32[1,3072]{1,0:T(1,128)S(1)}, f32[1,3072]{1,0:T(1,128)S(1)}, u32[]{:S(2)}, u32[]{:S(2)}) collective-permute-start(f32[1,3072]{1,0:T(1,128)S(1)} %collective-permute-done.27), channel_id=1, source_target_pairs={{1,0},{2,1},{3,2},{4,3},{5,4},{6,5},{7,6},{8,7},{9,8},{10,9},{11,1... | collective-permute-start | bytes 36872 | tf_op jit(solution)/shard_map/ppermute | solution.py:50
  279.2 6.0 %collective-permute-start.29 = (f32[]{:T(128)}, f32[]{:T(128)}, u32[]{:S(2)}, u32[]{:S(2)}) collective-permute-start(f32[]{:T(128)} %get-tuple-element.4), channel_id=1, source_target_pairs={{0,16},{16,0},{32,48},{48,32},{64,80},{80,64},{96,112},{112,96},{1... | collective-permute-start | bytes 20 | tf_op jit(solution)/shard_map/ppermute | solution.py:225
  286.4 2.5 collective-permute-start.30
  289.5 4.0 collective-permute-start.31
  294.1 2.6 collective-permute-start.32
  297.4 5.0 %collective-permute-start.33 = (f32[]{:T(128)}, f32[]{:T(128)}, u32[]{:S(2)}, u32[]{:S(2)}) collective-permute-start(f32[]{:T(128)} %add.273), channel_id=1, source_target_pairs={{0,2},{1,3},{2,0},{3,1},{4,6},{5,7},{6,4},{7,5},{8,10},{9,11},{10,... | collective-permute-start | bytes 20 | tf_op jit(solution)/shard_map/ppermute | solution.py:225
  303.1 2.5 collective-permute-start.34
  306.2 4.0 collective-permute-start.35
  311.4 8.7 %collective-permute-start.36 = (f32[]{:T(128)}, f32[]{:T(128)}, u32[]{:S(2)}, u32[]{:S(2)}) collective-permute-start(f32[]{:T(128)} %get-tuple-element.2), channel_id=1, source_target_pairs={{0,16},{16,0},{32,48},{48,32},{64,80},{80,64},{96,112},{112,96},{1... | collective-permute-start | bytes 20 | tf_op jit(solution)/shard_map/ppermute | solution.py:225
  321.4 2.5 collective-permute-start.37
  324.5 4.0 collective-permute-start.38
  329.1 2.5 collective-permute-start.39
  332.2 4.5 %collective-permute-start.40 = (f32[]{:T(128)}, f32[]{:T(128)}, u32[]{:S(2)}, u32[]{:S(2)}) collective-permute-start(f32[]{:T(128)} %add.281), channel_id=1, source_target_pairs={{0,2},{1,3},{2,0},{3,1},{4,6},{5,7},{6,4},{7,5},{8,10},{9,11},{10,... | collective-permute-start | bytes 20 | tf_op jit(solution)/shard_map/ppermute | solution.py:225
  340.4 4.0 collective-permute-start.42
  345.1 8.3 %collective-permute-start.43 = (f32[1,3072]{1,0:T(1,128)S(1)}, f32[1,3072]{1,0:T(1,128)S(1)}, u32[]{:S(2)}, u32[]{:S(2)}) collective-permute-start(f32[1,3072]{1,0:T(1,128)S(1)} %get-tuple-element.42), channel_id=1, source_target_pairs={{0,16},{16,32},{32,48},{48,64},{64,80},{80,96},{96,112},{112,0},{1... | collective-permute-start | bytes 36872 | tf_op jit(solution)/shard_map/ppermute | solution.py:44
  352.3 6.2 %collective-permute-start.45 = (f32[1,3072]{1,0:T(1,128)S(1)}, f32[1,3072]{1,0:T(1,128)S(1)}, u32[]{:S(2)}, u32[]{:S(2)}) collective-permute-start(f32[1,3072]{1,0:T(1,128)S(1)} %get-tuple-element.41), channel_id=1, source_target_pairs={{0,112},{16,0},{32,16},{48,32},{64,48},{80,64},{96,80},{112,96},{1... | collective-permute-start | bytes 36872 | tf_op jit(solution)/shard_map/ppermute | solution.py:44
  353.4 6.4 %collective-permute-start.44 = (f32[1,3072]{1,0:T(1,128)S(1)}, f32[1,3072]{1,0:T(1,128)S(1)}, u32[]{:S(2)}, u32[]{:S(2)}) collective-permute-start(f32[1,3072]{1,0:T(1,128)S(1)} %collective-permute-done.43), channel_id=1, source_target_pairs={{0,1},{1,2},{2,3},{3,4},{4,5},{5,6},{6,7},{7,8},{8,9},{9,10},{10,1... | collective-permute-start | bytes 36872 | tf_op jit(solution)/shard_map/ppermute | solution.py:50
  358.5 4.8 %collective-permute-start.46 = (f32[1,3072]{1,0:T(1,128)S(1)}, f32[1,3072]{1,0:T(1,128)S(1)}, u32[]{:S(2)}, u32[]{:S(2)}) collective-permute-start(f32[1,3072]{1,0:T(1,128)S(1)} %collective-permute-done.45), channel_id=1, source_target_pairs={{1,0},{2,1},{3,2},{4,3},{5,4},{6,5},{7,6},{8,7},{9,8},{10,9},{11,1... | collective-permute-start | bytes 36872 | tf_op jit(solution)/shard_map/ppermute | solution.py:50
  364.3 5.9 %collective-permute-start.47 = (f32[]{:T(128)}, f32[]{:T(128)}, u32[]{:S(2)}, u32[]{:S(2)}) collective-permute-start(f32[]{:T(128)} %fusion.57), channel_id=1, source_target_pairs={{0,16},{16,0},{32,48},{48,32},{64,80},{80,64},{96,112},{112,96},{1... | collective-permute-start | bytes 20 | tf_op jit(solution)/shard_map/ppermute | solution.py:225
  371.4 2.5 collective-permute-start.48
  374.5 4.0 collective-permute-start.49
  379.1 2.7 collective-permute-start.50
  382.5 4.9 %collective-permute-start.51 = (f32[]{:T(128)}, f32[]{:T(128)}, u32[]{:S(2)}, u32[]{:S(2)}) collective-permute-start(f32[]{:T(128)} %add.295), channel_id=1, source_target_pairs={{0,2},{1,3},{2,0},{3,1},{4,6},{5,7},{6,4},{7,5},{8,10},{9,11},{10,... | collective-permute-start | bytes 20 | tf_op jit(solution)/shard_map/ppermute | solution.py:225
  391.1 4.0 collective-permute-start.53
  (26 other events, 206.3 us)
